TPU v7x, 32 devices: a whole 2x2x4 slice. The times are simulated.
32 devices in a mesh: cp: 2 (over y), tp: 4 (over x, core), ep: 4 (over z).
Axes of the slice: x: 2, y: 2, z: 4, core: 2. Of those that a mesh axis runs over, the one named last changes fastest.
Arguments:
- query: bfloat16 [8, 512, 4096], P('ep', 'cp', 'tp'), may hold values from -6 to 6
- keys: bfloat16 [8, 512, 512], P('ep', 'cp', 'tp'), may hold values from -6 to 6
- values: bfloat16 [8, 512, 512], P('ep', 'cp', 'tp'), may hold values from -24 to 24
- segment_ids: int32 [8, 512], P('ep', 'cp'), may hold values from 0 to 3, never falling along the last dimension, each value on 1 to 256 neighbouring positions
- query_norm_gain: float32 [128], replicated, may hold values from 0.25 to 1.75
- key_norm_gain: float32 [128], replicated, may hold values from 0.25 to 1.75
- out_weight: bfloat16 [4096, 2048], P('tp', 'cp'), may hold values from -0.09375 to 0.09375
- residual: bfloat16 [8, 512, 2048], P('ep', 'cp'), may hold values from -3 to 3
- norm_gain: float32 [2048], replicated, may hold values from 0.25 to 1.75
- router_weight: bfloat16 [2048, 16], replicated, may hold values from -0.125 to 0.125
- expert_ids: int32 [8, 512, 8], P('ep', 'cp'), may hold values from 0 to 15, all different within a row; in each aligned block of 64 rows (0 to 63, 64 to 127, ..., all dimensions but the last counted through in order) at most 36 rows name the same one
- expert_gate: bfloat16 [16, 2048, 768], P(('tp', 'ep'), None, 'cp'), may hold values from -0.125 to 0.125
- expert_up: bfloat16 [16, 2048, 768], P(('tp', 'ep'), None, 'cp'), may hold values from -0.125 to 0.125
- expert_down: bfloat16 [16, 2048, 768], P(('tp', 'ep'), None, 'cp'), may hold values from -0.21875 to 0.21875
Outputs:
- layer_out: bfloat16 [8, 512, 2048], P('ep', ('cp', 'tp'))
Inputs may be any that keep to these rules, and one draw needn't show every extreme that they name: `segment_ids`: document numbers never fall along a sequence. `expert_ids`: each token names 8 different experts; in every aligned block of 64 positions of a sequence no expert is named by more than 36 tokens, a bound that some block reaches.
All inputs are finite; a program needn't handle non-finite values.
Results may differ from a plain program's by a relative error of at most 0.007.
Values may be sent and summed in bfloat16 or wider, within the bound.
No kernel may reach another device: no remote copies, remote signals or barrier semaphores. Data moves between devices by JAX's collectives and lax.ppermute only.
A program may use at most 128 MiB of HBM per device.

v0:
```python
import jax
import jax.numpy as jnp
from jax import lax
from jax.sharding import PartitionSpec as P

HEAD_WIDTH = 128


def root_mean_scale(entries, gain):
    mean_sq = jnp.mean(entries * entries, axis=-1, keepdims=True)
    return entries * lax.rsqrt(mean_sq + 1e-06) * gain


def capacity(share, top_count, experts):
    return min(
        share, max(2, share * top_count // experts + max(1, share * top_count // (8 * experts)))
    )


def slot_numbers(ids, experts):
    flat_ids = ids.reshape(-1)
    table = (flat_ids[:, None] == jnp.arange(experts, dtype=jnp.int32)[None, :]).astype(jnp.int32)
    before = jnp.cumsum(table, axis=0) - table
    return jnp.sum(before * table, axis=1).reshape(ids.shape)


def route(state, ids, norm_gain, router_weight):
    normed = root_mean_scale(state, norm_gain).astype(jnp.bfloat16)
    logits = jnp.dot(normed, router_weight, preferred_element_type=jnp.float32)
    experts = router_weight.shape[1]
    picks = ids[:, :, None] == jnp.arange(experts, dtype=jnp.int32)[None, None, :]
    chosen = jnp.sum(jnp.where(picks, logits[:, None, :], jnp.float32(0.0)), axis=-1)
    raised = jnp.exp(chosen)
    return (normed, raised / jnp.sum(raised, axis=-1, keepdims=True))


def expert_rows(received, full_gate, full_up, full_down):
    width = received.shape[-1]
    flat_rows = received.reshape(-1, width)
    gate_act = jnp.dot(flat_rows, full_gate[0], preferred_element_type=jnp.float32)
    up_act = jnp.dot(flat_rows, full_up[0], preferred_element_type=jnp.float32)
    hidden_act = (jax.nn.silu(gate_act) * up_act).astype(jnp.bfloat16)
    served = jnp.einsum(
        "rf,df->rd", hidden_act, full_down[0], preferred_element_type=jnp.float32
    ).astype(jnp.bfloat16)
    return served.reshape(received.shape)


def shards(
    query,
    keys,
    values,
    segment_ids,
    query_norm_gain,
    key_norm_gain,
    out_weight,
    residual,
    norm_gain,
    router_weight,
    expert_ids,
    expert_gate,
    expert_up,
    expert_down,
):
    packs = query.shape[0]
    row_count = query.shape[1]
    head_count = query.shape[2] // HEAD_WIDTH
    width = residual.shape[2]
    experts = router_weight.shape[1]
    top_count = expert_ids.shape[2]
    score_scale = HEAD_WIDTH ** (-0.5)
    query_rows_normed = root_mean_scale(
        query.astype(jnp.float32).reshape(packs, row_count, head_count, HEAD_WIDTH), query_norm_gain
    ).astype(jnp.bfloat16)
    key_rows_normed = root_mean_scale(keys.astype(jnp.float32), key_norm_gain).astype(jnp.bfloat16)
    own_docs = segment_ids.astype(jnp.bfloat16)
    key_piece = lax.all_gather(key_rows_normed, "cp", axis=1, tiled=True)
    value_piece = lax.all_gather(values, "cp", axis=1, tiled=True)
    doc_piece = lax.all_gather(own_docs, "cp", axis=1, tiled=True)
    scores = (
        jnp.einsum(
            "pshd,pnd->phsn", query_rows_normed, key_piece, preferred_element_type=jnp.float32
        )
        * score_scale
    )
    same_doc = own_docs[:, :, None] == doc_piece[:, None, :]
    probs = jnp.where(same_doc[:, None], jnp.exp(scores), jnp.float32(0.0))
    denom = jnp.sum(probs, axis=-1)
    probs_b = probs.astype(jnp.bfloat16)
    summed = jnp.einsum("phsn,pnd->pshd", probs_b, value_piece, preferred_element_type=jnp.float32)
    denom, summed = (denom, summed)
    attn = (
        (summed / jnp.transpose(denom, (0, 2, 1))[:, :, :, None])
        .astype(jnp.bfloat16)
        .reshape(packs * row_count, head_count * HEAD_WIDTH)
    )
    partial_proj = jnp.dot(
        attn,
        lax.all_gather(out_weight, "cp", axis=1, tiled=True),
        preferred_element_type=jnp.float32,
    ).reshape(packs, row_count, width)
    full_gate, full_up, full_down = (
        lax.all_gather(expert_gate, "cp", axis=2, tiled=True),
        lax.all_gather(expert_up, "cp", axis=2, tiled=True),
        lax.all_gather(expert_down, "cp", axis=2, tiled=True),
    )
    share = row_count // lax.axis_size("tp")
    tp_index = lax.axis_index("tp")
    cap = capacity(share, top_count, experts)
    projected = lax.psum_scatter(partial_proj, "tp", scatter_dimension=1, tiled=True)
    first_row = tp_index * share
    state = lax.dynamic_slice_in_dim(residual, first_row, share, 1).astype(jnp.float32) + projected
    local_ids = lax.dynamic_slice_in_dim(expert_ids, first_row, share, 1).reshape(
        packs * share, top_count
    )
    normed, gates = route(state.reshape(packs * share, width), local_ids, norm_gain, router_weight)
    dev_cap = packs * cap
    slots = slot_numbers(local_ids, experts)
    target = (local_ids * dev_cap + slots).reshape(-1)
    sent_rows = jnp.broadcast_to(normed[:, None, :], (packs * share, top_count, width)).reshape(
        -1, width
    )
    buffer = (
        jnp.zeros((experts * dev_cap, width), jnp.bfloat16)
        .at[target]
        .set(sent_rows)
        .reshape(experts, dev_cap, width)
    )
    served = expert_rows(
        lax.all_to_all(buffer, ("tp", "ep"), split_axis=0, concat_axis=0, tiled=True),
        full_gate,
        full_up,
        full_down,
    )
    back = lax.all_to_all(served, ("tp", "ep"), split_axis=0, concat_axis=0, tiled=True)
    picked = back.reshape(experts * dev_cap, width)[target].reshape(packs * share, top_count, width)
    mixture = jnp.sum(gates[:, :, None] * picked.astype(jnp.float32), axis=1)
    layer_out = (state + mixture.reshape(packs, share, width)).astype(jnp.bfloat16)
    return layer_out


def solution(mesh):
    return jax.shard_map(
        shards,
        mesh=mesh,
        in_specs=(
            P("ep", "cp", "tp"),
            P("ep", "cp", "tp"),
            P("ep", "cp", "tp"),
            P("ep", "cp"),
            P(),
            P(),
            P("tp", "cp"),
            P("ep", "cp", None),
            P(),
            P(),
            P("ep", "cp", None),
            P(("tp", "ep"), None, "cp"),
            P(("tp", "ep"), None, "cp"),
            P(("tp", "ep"), None, "cp"),
        ),
        out_specs=P("ep", ("cp", "tp"), None),
        check_vma=False,
    )
```

profile of v0, /device:TPU:0, one launch (start us, length us, event | category | flops | bytes accessed | tf_op | source)
XLA Modules:
  0.0 424.7 jit_solution(739500518917911366)
XLA Ops:
  8.0 1.5 copy.74
  10.5 5.2 %all_gather.21 = bf16[2,512]{1,0:T(2,128)(2,1)S(1)} all-gather(bf16[2,256]{1,0:T(2,128)(2,1)S(1)} %convert_element_type.52), channel_id=1, replica_groups=mesh['cp'=2,'tp'=4,'ep'=4] {'cp'}, dimensions={1}, use_global_device_ids=true | all-gather | bytes 3072 | tf_op jit(solution)/shard_map/all_gather | solution.py:79
  16.0 5.7 %all_gather.22 = bf16[2,512,128]{2,1,0:T(8,128)(2,1)S(1)} all-gather(bf16[2,256,128]{2,1,0:T(8,128)(2,1)S(1)} %fusion.31), channel_id=1, replica_groups=mesh['cp'=2,'tp'=4,'ep'=4] {'cp'}, dimensions={1}, use_global_device_ids=true | all-gather | bytes 393216 | tf_op jit(solution)/shard_map/all_gather | solution.py:77
  21.6 8.7 %all_gather.23 = bf16[2,512,128]{1,2,0:T(8,128)(2,1)S(1)} all-gather(bf16[2,256,128]{1,2,0:T(8,128)(2,1)S(1)} %copy.60), channel_id=1, replica_groups=mesh['cp'=2,'tp'=4,'ep'=4] {'cp'}, dimensions={1}, use_global_device_ids=true | all-gather | bytes 393216 | tf_op jit(solution)/shard_map/all_gather | solution.py:78
  31.3 2.2 fusion.1
  33.5 1.7 fusion.21
  35.2 35.5 %all-gather.5.cloned.1.call-done = bf16[1024,2048]{1,0:T(8,128)(2,1)} async-done(((bf16[1024,1024]{1,0:T(8,128)(2,1)}), bf16[1024,2048]{1,0:T(8,128)(2,1)}) %all-gather.5.cloned.1.call-update) | async-done | bytes 4194320 | tf_op jit(solution)/shard_map/all_gather | solution.py:99
  70.7 6.5 %fusion.7 = f32[2,256,2048]{2,1,0:T(8,128)} fusion(bf16[2,256,1024]{1,2,0:T(8,128)(2,1)S(1)} %bitcast.104, bf16[1024,2048]{1,0:T(8,128)(2,1)} %all-gather.5.cloned.1.call-done), kind=kOutput, calls=%fused_computation.11 | convolution fusion | flops 2147483648 | bytes 9437184 | tf_op jit(solution)/shard_map/dot_general | solution.py:97
  78.3 4.5 %reduce-window.6 = s32[16,8,128]{2,1,0:T(8,128)S(1)} reduce-window(s32[16,8,128]{2,1,0:T(8,128)S(1)} %fusion.37, s32[]{:T(128)} %constant.14.clone.1), window={size=1x1x128 pad=0_0x0_0x127_0}, to_apply=%region_7.8 | reduce-window | flops 2080768 | bytes 131076 | tf_op jit(solution)/shard_map/reduce-window
  83.5 39.1 %reduce-scatter.2.cloned.1.call-done = f32[2,64,2048]{2,1,0:T(8,128)} async-done(((f32[2,256,2048]{2,1,0:T(8,128)}), f32[2,64,2048]{2,1,0:T(8,128)}) %reduce-scatter.2.cloned.1.call-update) | async-done | bytes 1048592 | tf_op jit(solution)/shard_map/reduce_scatter | solution.py:110
  122.6 1.6 multiply_reduce_fusion
  124.5 9.4 %scatter_custom_fusion = bf16[1152,2048]{1,0:T(8,128)(2,1)} fusion(s32[1024]{0:T(1024)S(1)} %bitcast.109, bf16[]{:T(256)} %constant.37.clone.1, bf16[128,2048]{1,0:T(8,128)(2,1)S(1)} %fusion.26), kind=kCustom, calls=%fused_computation.9 | custom fusion | bytes 5242882 | tf_op jit(solution)/shard_map/scatter | solution.py:126
  133.8 4.8 %all-to-all-start = ((bf16[16,72,2048]{2,1,0:T(8,128)(2,1)}), bf16[16,72,2048]{2,1,0:T(8,128)(2,1)}, u32[]{:S(2)}, u32[]{:S(2)}) async-start(bf16[16,72,2048]{2,1,0:T(8,128)(2,1)} %bitcast.101), calls=%async_computation.1 | async-start | bytes 9437184 | tf_op jit(solution)/shard_map/all_to_all | solution.py:130
  140.5 46.8 %all-gather.7.cloned.1.call-done = bf16[1,2048,768]{2,1,0:T(8,128)(2,1)} async-done(((bf16[1,2048,384]{2,1,0:T(8,128)(2,1)}), bf16[1,2048,768]{2,1,0:T(8,128)(2,1)}) %all-gather.7.cloned.1.call-update) | async-done | bytes 3145744 | tf_op jit(solution)/shard_map/all_gather | solution.py:103
  187.3 57.0 %all-to-all-done = bf16[16,72,2048]{2,1,0:T(8,128)(2,1)} async-done(((bf16[16,72,2048]{2,1,0:T(8,128)(2,1)}), bf16[16,72,2048]{2,1,0:T(8,128)(2,1)}, u32[]{:S(2)}, u32[]{:S(2)}) %all-to-all-start) | async-done | bytes 4718624 | tf_op jit(solution)/shard_map/all_to_all | solution.py:130
  244.3 9.4 %fusion.15 = f32[1152,768]{1,0:T(8,128)} fusion(bf16[1152,2048]{1,0:T(8,128)(2,1)} %bitcast.16, bf16[1,2048,768]{2,1,0:T(8,128)(2,1)} %all-gather.7.cloned.1.call-done), kind=kOutput, calls=%fused_computation.20 | convolution fusion | flops 3623878656 | bytes 11403264 | tf_op jit(solution)/shard_map/dot_general | solution.py:40
  253.7 8.5 %fusion.12 = bf16[1152,768]{1,0:T(8,128)(2,1)S(1)} fusion(bf16[1152,2048]{1,0:T(8,128)(2,1)} %bitcast.16, f32[1152,768]{1,0:T(8,128)} %fusion.15, bf16[1,2048,768]{2,1,0:T(8,128)(2,1)} %all-gather.9.cloned.1.call-done), kind=kOutput, calls=%fused_computation.17 | convolution fusion | flops 3629187072 | bytes 13172736 | tf_op jit(solution)/shard_map/dot_general | solution.py:41
  262.2 18.0 %all-gather.11.cloned.1.call-done = bf16[1,2048,768]{2,1,0:T(8,128)(2,1)} async-done(((bf16[1,2048,384]{2,1,0:T(8,128)(2,1)}), bf16[1,2048,768]{2,1,0:T(8,128)(2,1)}) %all-gather.11.cloned.1.call-update) | async-done | bytes 3145744 | tf_op jit(solution)/shard_map/all_gather | solution.py:105
  280.1 7.4 %convolution_convert_fusion = bf16[1152,2048]{1,0:T(8,128)(2,1)} fusion(bf16[1152,768]{1,0:T(8,128)(2,1)S(1)} %fusion.12, bf16[1,2048,768]{2,1,0:T(8,128)(2,1)} %all-gather.11.cloned.1.call-done), kind=kOutput, calls=%fused_computation.5 | convolution fusion | flops 3626237952 | bytes 9633792 | tf_op jit(solution)/shard_map/rf,df->rd/dot_general | solution.py:43
  287.6 5.7 %all-to-all-start.1 = ((bf16[16,72,2048]{2,1,0:T(8,128)(2,1)}), bf16[16,72,2048]{2,1,0:T(8,128)(2,1)}, u32[]{:S(2)}, u32[]{:S(2)}) async-start(bf16[16,72,2048]{2,1,0:T(8,128)(2,1)} %bitcast.102), calls=%async_computation.2 | async-start | bytes 9437184 | tf_op jit(solution)/shard_map/all_to_all | solution.py:135
  293.8 105.2 %all-to-all-done.1 = bf16[16,72,2048]{2,1,0:T(8,128)(2,1)} async-done(((bf16[16,72,2048]{2,1,0:T(8,128)(2,1)}), bf16[16,72,2048]{2,1,0:T(8,128)(2,1)}, u32[]{:S(2)}, u32[]{:S(2)}) %all-to-all-start.1) | async-done | bytes 4718624 | tf_op jit(solution)/shard_map/all_to_all | solution.py:135
  398.9 11.8 %gather_fusion = bf16[1024,2048]{1,0:T(8,128)(2,1)} fusion(bf16[1152,2048]{1,0:T(8,128)(2,1)} %bitcast.21, s32[1024]{0:T(1024)S(1)} %broadcast_clamp_fusion), kind=kCustom, calls=%fused_computation | custom fusion | bytes 8392704 | tf_op jit(solution)/shard_map/gather | solution.py:136
  410.7 6.5 %fusion = f32[128,2048]{1,0:T(8,128)S(1)} fusion(bf16[1024,2048]{1,0:T(8,128)(2,1)} %gather_fusion, f32[128,8]{1,0:T(8,128)S(1)} %copy.64), kind=kLoop, calls=%fused_computation.3 | loop fusion | flops 6029312 | bytes 5246976 | tf_op jit(solution)/shard_map/reduce_sum | solution.py:137
  417.3 0.9 add_convert_fusion
  (62 shorter events, 8.0 us)
Async XLA Ops:
  6.5 286.8 %copy-start = (bf16[2048,16]{0,1:T(8,128)(2,1)S(1)}, bf16[2048,16]{0,1:T(8,128)(2,1)}, u32[]{:S(2)}) copy-start(bf16[2048,16]{0,1:T(8,128)(2,1)} %param.23) | copy-start | bytes 196612
  6.5 3.8 copy-start.2
  6.5 9.1 %copy-start.1 = (bf16[2,256,128]{2,1,0:T(8,128)(2,1)S(1)}, bf16[2,256,128]{2,1,0:T(8,128)(2,1)}, u32[]{:S(2)}) copy-start(bf16[2,256,128]{2,1,0:T(8,128)(2,1)} %param.15) | copy-start | bytes 393220
  6.5 9.3 %copy-start.5 = (f32[128]{0:T(128)S(1)}, f32[128]{0:T(128)}, u32[]{:S(2)}) copy-start(f32[128]{0:T(128)} %param.19) | copy-start | bytes 1540
  6.5 64.2 %all-gather.5.cloned.1.call-start = ((), (), s32[]{:S(2)}) async-start(), calls=%async_computation.3 | async-start | bytes 6291456 | tf_op jit(solution)/shard_map/all_gather | solution.py:99
  7.3 23.3 %copy-start.6 = (f32[128]{0:T(128)S(1)}, f32[128]{0:T(128)}, u32[]{:S(2)}) copy-start(f32[128]{0:T(128)} %param.18) | copy-start | bytes 1540
  7.3 115.3 %reduce-scatter.2.cloned.1.call-start = ((), (), s32[]{:S(2)}) async-start(), calls=%async_computation.4 | async-start | bytes 5242880 | tf_op jit(solution)/shard_map/reduce_scatter | solution.py:110
  77.2 0.7 copy-start.4
  77.2 47.1 %copy-start.3 = (f32[2048]{0:T(1024)S(1)}, f32[2048]{0:T(1024)}, u32[]{:S(2)}) copy-start(f32[2048]{0:T(1024)} %param.22) | copy-start | bytes 24580
  133.8 110.5 %all-to-all-start = ((bf16[16,72,2048]{2,1,0:T(8,128)(2,1)}), bf16[16,72,2048]{2,1,0:T(8,128)(2,1)}, u32[]{:S(2)}, u32[]{:S(2)}) async-start(bf16[16,72,2048]{2,1,0:T(8,128)(2,1)} %bitcast.101), calls=%async_computation.1 | async-start | bytes 9437184 | tf_op jit(solution)/shard_map/all_to_all | solution.py:130
  138.6 48.7 %all-gather.7.cloned.1.call-start = ((), (), s32[]{:S(2)}) async-start(), calls=%async_computation.5 | async-start | bytes 4718592 | tf_op jit(solution)/shard_map/all_gather | solution.py:103
  139.3 114.3 %all-gather.9.cloned.1.call-start = ((), (), s32[]{:S(2)}) async-start(), calls=%async_computation.6 | async-start | bytes 4718592 | tf_op jit(solution)/shard_map/all_gather | solution.py:104
  139.9 140.2 %all-gather.11.cloned.1.call-start = ((), (), s32[]{:S(2)}) async-start(), calls=%async_computation.7 | async-start | bytes 4718592 | tf_op jit(solution)/shard_map/all_gather | solution.py:105
  287.6 111.3 %all-to-all-start.1 = ((bf16[16,72,2048]{2,1,0:T(8,128)(2,1)}), bf16[16,72,2048]{2,1,0:T(8,128)(2,1)}, u32[]{:S(2)}, u32[]{:S(2)}) async-start(bf16[16,72,2048]{2,1,0:T(8,128)(2,1)} %bitcast.102), calls=%async_computation.2 | async-start | bytes 9437184 | tf_op jit(solution)/shard_map/all_to_all | solution.py:135
Sparse Core Ops, SparseCore 0:
  8.9 61.7 all-gather.4
  77.4 45.2 reduce-scatter.1
  141.1 46.1 all-gather.6
  188.7 44.9 all-gather.8
  235.2 44.9 all-gather.10
where the time goes:
time: 425 us
  waiting for transfers between devices  304 us (72%)
  matrix products  35.9 us (8%)
  local copies, waits for them, and re-layouts  24.7 us (6%)
  blocking collectives  19.5 us (5%)
  other arithmetic  16.6 us (4%)
  between operations  13.4 us (3%)
  starting transfers between devices  10.6 us (2%)
    all_to_all x1, waiting for transfers between devices, shards(): lax.all_to_all(served, ('tp', 'ep'), split_axis=0, concat_axis=0, tiled=T...  105 us
    all_to_all x1, waiting for transfers between devices, shards(): lax.all_to_all(buffer, ('tp', 'ep'), split_axis=0, concat_axis=0, tiled=T...  57 us
    all_gather x1, waiting for transfers between devices, shards(): lax.all_gather(expert_gate, 'cp', axis=2, tiled=True)  46.8 us
    reduce_scatter x1, waiting for transfers between devices, shards(): lax.psum_scatter(partial_proj, 'tp', scatter_dimension=1, tiled=True)  39.1 us
    all_gather x1, waiting for transfers between devices, shards(): lax.all_gather(out_weight, 'cp', axis=1, tiled=True)  35.5 us
    all_gather x1, waiting for transfers between devices, shards(): lax.all_gather(expert_down, 'cp', axis=2, tiled=True)  18 us
    gather x1, local copies, waits for them, and re-layouts, shards(): back.reshape(experts * dev_cap, width)[target]  11.8 us
    dot_general x1, matrix products, expert_rows(): jnp.dot(flat_rows, full_gate[0], preferred_element_type=jnp.float32)  9.4 us
  transfers between devices with their start and end apart: 7, of which 6 were waited for; matrix products, arithmetic and copies ran while one was open for 8% of the time, Pallas kernels for 0%

commit v1 on v0

--- a/solution.py
+++ b/solution.py
@@ -4,6 +4,22 @@
 from jax.sharding import PartitionSpec as P
 
 HEAD_WIDTH = 128
+
+
+def exchange_in_pairs(x, axis, split, join):
+    ways, here = (lax.axis_size(axis), lax.axis_index(axis))
+    width = x.shape[split] // ways
+    lengths = list(x.shape)
+    lengths[split] = width
+    height = lengths[join]
+    lengths[join] = height * ways
+    full = jnp.zeros(lengths, x.dtype)
+    for mask in range(ways):
+        part = lax.dynamic_slice_in_dim(x, (here ^ mask) * width, width, axis=split)
+        if mask:
+            part = lax.ppermute(part, axis, [(d, d ^ mask) for d in range(ways)])
+        full = lax.dynamic_update_slice_in_dim(full, part, (here ^ mask) * height, axis=join)
+    return full
 
 
 def root_mean_scale(entries, gain):
@@ -127,10 +143,7 @@
         .reshape(experts, dev_cap, width)
     )
     served = expert_rows(
-        lax.all_to_all(buffer, ("tp", "ep"), split_axis=0, concat_axis=0, tiled=True),
-        full_gate,
-        full_up,
-        full_down,
+        exchange_in_pairs(buffer, ("tp", "ep"), 0, 0), full_gate, full_up, full_down
     )
     back = lax.all_to_all(served, ("tp", "ep"), split_axis=0, concat_axis=0, tiled=True)
     picked = back.reshape(experts * dev_cap, width)[target].reshape(packs * share, top_count, width)

time: 425 us -> 411 us (0.967)
  waiting for transfers between devices: 304 us -> 228 us
  starting transfers between devices: 10.6 us -> 54.6 us
  local copies, waits for them, and re-layouts: 24.7 us -> 43.3 us
    all_to_all x1 -> x0, waiting for transfers between devices: 57 us -> none  [shards(): lax.all_to_all(buffer, ('tp', 'ep'), split_axis=0, concat_axis=0, tiled=T...]
    all_gather x1, waiting for transfers between devices: 46.8 us -> 0.01 us  [shards(): lax.all_gather(expert_gate, 'cp', axis=2, tiled=True)]
    ppermute x0 -> x15, waiting for transfers between devices: none -> 45.3 us  [exchange_in_pairs(): part = lax.ppermute(part, axis, [(d, d ^ mask) for d in range(ways)])]
    ppermute x0 -> x15, starting transfers between devices: none -> 44.7 us  [exchange_in_pairs(): part = lax.ppermute(part, axis, [(d, d ^ mask) for d in range(ways)])]
    all_gather x1, waiting for transfers between devices: 18 us -> 1.5 us  [shards(): lax.all_gather(expert_down, 'cp', axis=2, tiled=True)]
    dynamic_update_slice x0 -> x15, local copies, waits for them, and re-layouts: none -> 13 us  [exchange_in_pairs(): lax.dynamic_update_slice_in_dim(full, part, (here ^ mask) * height, axis=...]
    all_to_all x1 -> x0, starting transfers between devices: 4.77 us -> none  [shards(): lax.all_to_all(buffer, ('tp', 'ep'), split_axis=0, concat_axis=0, tiled=T...]
  transfers between devices with their start and end apart: 7 -> 21, of which waited for: 6 -> 10; matrix products, arithmetic and copies ran while one was open for 8% -> 14% of each run, Pallas kernels for 0% -> 0%
where the time goes in v1:
time: 411 us
  waiting for transfers between devices  228 us (55%)
  starting transfers between devices  54.6 us (13%)
  local copies, waits for them, and re-layouts  43.3 us (11%)
  matrix products  35.5 us (9%)
  blocking collectives  19.4 us (5%)
  other arithmetic  16.6 us (4%)
  between operations  13.6 us (3%)
    all_to_all x1, waiting for transfers between devices, shards(): lax.all_to_all(served, ('tp', 'ep'), split_axis=0, concat_axis=0, tiled=T...  105 us
    ppermute x15, waiting for transfers between devices, exchange_in_pairs(): part = lax.ppermute(part, axis, [(d, d ^ mask) for d in range(ways)])  45.3 us
    ppermute x15, starting transfers between devices, exchange_in_pairs(): part = lax.ppermute(part, axis, [(d, d ^ mask) for d in range(ways)])  44.7 us
    reduce_scatter x1, waiting for transfers between devices, shards(): lax.psum_scatter(partial_proj, 'tp', scatter_dimension=1, tiled=True)  38.4 us
    all_gather x1, waiting for transfers between devices, shards(): lax.all_gather(out_weight, 'cp', axis=1, tiled=True)  35.6 us
    dynamic_update_slice x15, local copies, waits for them, and re-layouts, exchange_in_pairs(): lax.dynamic_update_slice_in_dim(full, part, (here ^ mask) * height, axis=...  13 us
    gather x1, local copies, waits for them, and re-layouts, shards(): back.reshape(experts * dev_cap, width)[target]  11.8 us
    all_to_all x1, starting transfers between devices, shards(): lax.all_to_all(served, ('tp', 'ep'), split_axis=0, concat_axis=0, tiled=T...  9.78 us
  transfers between devices with their start and end apart: 21, of which 10 were waited for; matrix products, arithmetic and copies ran while one was open for 14% of the time, Pallas kernels for 0%

profile of v1, /device:TPU:0, one launch (start us, length us, event | category | flops | bytes accessed | tf_op | source)
XLA Modules:
  0.0 410.9 jit_solution(6522443817320301052)
XLA Ops:
  10.5 5.2 %all_gather.21 = bf16[2,512]{1,0:T(2,128)(2,1)S(1)} all-gather(bf16[2,256]{1,0:T(2,128)(2,1)S(1)} %convert_element_type.52), channel_id=1, replica_groups=mesh['cp'=2,'tp'=4,'ep'=4] {'cp'}, dimensions={1}, use_global_device_ids=true | all-gather | bytes 3072 | tf_op jit(solution)/shard_map/all_gather | solution.py:95
  16.0 5.7 %all_gather.22 = bf16[2,512,128]{2,1,0:T(8,128)(2,1)S(1)} all-gather(bf16[2,256,128]{2,1,0:T(8,128)(2,1)S(1)} %fusion.33), channel_id=1, replica_groups=mesh['cp'=2,'tp'=4,'ep'=4] {'cp'}, dimensions={1}, use_global_device_ids=true | all-gather | bytes 393216 | tf_op jit(solution)/shard_map/all_gather | solution.py:93
  21.6 8.5 %all_gather.23 = bf16[2,512,128]{1,2,0:T(8,128)(2,1)S(1)} all-gather(bf16[2,256,128]{1,2,0:T(8,128)(2,1)S(1)} %copy.60), channel_id=1, replica_groups=mesh['cp'=2,'tp'=4,'ep'=4] {'cp'}, dimensions={1}, use_global_device_ids=true | all-gather | bytes 393216 | tf_op jit(solution)/shard_map/all_gather | solution.py:94
  35.1 35.6 %all-gather.5.cloned.1.call-done = bf16[1024,2048]{1,0:T(8,128)(2,1)} async-done(((bf16[1024,1024]{1,0:T(8,128)(2,1)}), bf16[1024,2048]{1,0:T(8,128)(2,1)}) %all-gather.5.cloned.1.call-update) | async-done | bytes 4194320 | tf_op jit(solution)/shard_map/all_gather | solution.py:115
  70.7 6.5 %fusion.7 = f32[2,256,2048]{2,1,0:T(8,128)} fusion(bf16[2,256,1024]{1,2,0:T(8,128)(2,1)S(1)} %bitcast.108, bf16[1024,2048]{1,0:T(8,128)(2,1)} %all-gather.5.cloned.1.call-done), kind=kOutput, calls=%fused_computation.11 | convolution fusion | flops 2147483648 | bytes 9437184 | tf_op jit(solution)/shard_map/dot_general | solution.py:113
  79.1 4.5 %reduce-window.6 = s32[16,8,128]{2,1,0:T(8,128)S(1)} reduce-window(s32[16,8,128]{2,1,0:T(8,128)S(1)} %fusion.39, s32[]{:T(128)} %constant.30.clone.1), window={size=1x1x128 pad=0_0x0_0x127_0}, to_apply=%region_7.8 | reduce-window | flops 2080768 | bytes 131076 | tf_op jit(solution)/shard_map/reduce-window
  84.4 38.4 %reduce-scatter.2.cloned.1.call-done = f32[2,64,2048]{2,1,0:T(8,128)} async-done(((f32[2,256,2048]{2,1,0:T(8,128)}), f32[2,64,2048]{2,1,0:T(8,128)}) %reduce-scatter.2.cloned.1.call-update) | async-done | bytes 1048592 | tf_op jit(solution)/shard_map/reduce_scatter | solution.py:126
  124.6 9.3 %scatter_custom_fusion = bf16[1152,2048]{1,0:T(8,128)(2,1)} fusion(s32[1024]{0:T(1024)S(1)} %bitcast.113, bf16[]{:T(256)} %constant.14.clone.1, bf16[128,2048]{1,0:T(8,128)(2,1)S(1)} %fusion.28), kind=kCustom, calls=%fused_computation.9 | custom fusion | bytes 5242882 | tf_op jit(solution)/shard_map/scatter | solution.py:142
  141.8 2.4 collective-permute-start.1
  145.5 10.5 %collective-permute-done = bf16[1,72,2048]{2,1,0:T(8,128)(2,1)} collective-permute-done((bf16[1,72,2048]{2,1,0:T(8,128)(2,1)}, bf16[1,72,2048]{2,1,0:T(8,128)(2,1)}, u32[]{:S(2)}, u32[]{:S(2)}) %collective-permute-start) | collective-permute-done | bytes 294944 | tf_op jit(solution)/shard_map/ppermute | solution.py:20
  157.7 8.0 %collective-permute-done.1 = bf16[1,72,2048]{2,1,0:T(8,128)(2,1)} collective-permute-done((bf16[1,72,2048]{2,1,0:T(8,128)(2,1)}, bf16[1,72,2048]{2,1,0:T(8,128)(2,1)}, u32[]{:S(2)}, u32[]{:S(2)}) %collective-permute-start.1) | collective-permute-done | bytes 294944 | tf_op jit(solution)/shard_map/ppermute | solution.py:20
  168.7 18.6 %collective-permute-start.8 = (bf16[1,72,2048]{2,1,0:T(8,128)(2,1)}, bf16[1,72,2048]{2,1,0:T(8,128)(2,1)S(1)}, u32[]{:S(2)}, u32[]{:S(2)}) collective-permute-start(bf16[1,72,2048]{2,1,0:T(8,128)(2,1)} %get-tuple-element.15), channel_id=1, source_target_pairs={{0,9},{1,8},{2,11},{3,10},{4,13},{5,12},{6,15},{7,14},{8,1},{9,0},... | collective-permute-start | bytes 884744 | tf_op jit(solution)/shard_map/ppermute | solution.py:20
  194.5 10.0 %collective-permute-start.11 = (bf16[1,72,2048]{2,1,0:T(8,128)(2,1)S(1)}, bf16[1,72,2048]{2,1,0:T(8,128)(2,1)S(1)}, u32[]{:S(2)}, u32[]{:S(2)}) collective-permute-start(bf16[1,72,2048]{2,1,0:T(8,128)(2,1)S(1)} %get-tuple-element.12), channel_id=1, source_target_pairs={{0,12},{1,13},{2,14},{3,15},{4,8},{5,9},{6,10},{7,11},{8,4},{9,5},... | collective-permute-start | bytes 884744 | tf_op jit(solution)/shard_map/ppermute | solution.py:20
  205.2 6.3 %collective-permute-start.12 = (bf16[1,72,2048]{2,1,0:T(8,128)(2,1)S(1)}, bf16[1,72,2048]{2,1,0:T(8,128)(2,1)S(1)}, u32[]{:S(2)}, u32[]{:S(2)}) collective-permute-start(bf16[1,72,2048]{2,1,0:T(8,128)(2,1)S(1)} %get-tuple-element.11), channel_id=1, source_target_pairs={{0,13},{1,12},{2,15},{3,14},{4,9},{5,8},{6,11},{7,10},{8,5},{9,4},... | collective-permute-start | bytes 884744 | tf_op jit(solution)/shard_map/ppermute | solution.py:20
  213.5 2.8 collective-permute-done.9
  217.9 5.8 %collective-permute-done.11 = bf16[1,72,2048]{2,1,0:T(8,128)(2,1)S(1)} collective-permute-done((bf16[1,72,2048]{2,1,0:T(8,128)(2,1)S(1)}, bf16[1,72,2048]{2,1,0:T(8,128)(2,1)S(1)}, u32[]{:S(2)}, u32[]{:S(2)}) %collective-permute-start.11) | collective-permute-done | bytes 294944 | tf_op jit(solution)/shard_map/ppermute | solution.py:20
  225.1 16.7 %collective-permute-done.13 = bf16[1,72,2048]{2,1,0:T(8,128)(2,1)S(1)} collective-permute-done((bf16[1,72,2048]{2,1,0:T(8,128)(2,1)S(1)}, bf16[1,72,2048]{2,1,0:T(8,128)(2,1)S(1)}, u32[]{:S(2)}, u32[]{:S(2)}) %collective-permute-start.13) | collective-permute-done | bytes 294944 | tf_op jit(solution)/shard_map/ppermute | solution.py:20
  243.3 8.9 %fusion.17 = f32[1152,768]{1,0:T(8,128)} fusion(bf16[1152,2048]{1,0:T(8,128)(2,1)} %bitcast.105, bf16[1,2048,768]{2,1,0:T(8,128)(2,1)} %all-gather.7.cloned.1.call-done), kind=kOutput, calls=%fused_computation.20 | convolution fusion | flops 3623878656 | bytes 11403264 | tf_op jit(solution)/shard_map/dot_general | solution.py:56
  252.2 8.5 %multiply_convert_fusion = bf16[1152,768]{1,0:T(8,128)(2,1)S(1)} fusion(f32[1152,768]{1,0:T(8,128)} %fusion.17, bf16[1152,2048]{1,0:T(8,128)(2,1)} %bitcast.106, bf16[1,2048,768]{2,1,0:T(8,128)(2,1)} %all-gather.9.cloned.1.call-done), kind=kOutput, calls=%fused_computation.16 | convolution fusion | flops 3629187072 | bytes 13172736 | tf_op jit(solution)/shard_map/dot_general | solution.py:57
  262.2 7.4 %convolution_convert_fusion = bf16[1152,2048]{1,0:T(8,128)(2,1)} fusion(bf16[1152,768]{1,0:T(8,128)(2,1)S(1)} %multiply_convert_fusion, bf16[1,2048,768]{2,1,0:T(8,128)(2,1)} %all-gather.11.cloned.1.call-done), kind=kOutput, calls=%fused_computation.5 | convolution fusion | flops 3626237952 | bytes 9633792 | tf_op jit(solution)/shard_map/rf,df->rd/dot_general | solution.py:59
  269.7 9.8 %all-to-all-start = ((bf16[16,72,2048]{2,1,0:T(8,128)(2,1)}), bf16[16,72,2048]{2,1,0:T(8,128)(2,1)}, u32[]{:S(2)}, u32[]{:S(2)}) async-start(bf16[16,72,2048]{2,1,0:T(8,128)(2,1)} %bitcast.104), calls=%async_computation.1 | async-start | bytes 9437184 | tf_op jit(solution)/shard_map/all_to_all | solution.py:148
  280.0 105.2 %all-to-all-done = bf16[16,72,2048]{2,1,0:T(8,128)(2,1)} async-done(((bf16[16,72,2048]{2,1,0:T(8,128)(2,1)}), bf16[16,72,2048]{2,1,0:T(8,128)(2,1)}, u32[]{:S(2)}, u32[]{:S(2)}) %all-to-all-start) | async-done | bytes 4718624 | tf_op jit(solution)/shard_map/all_to_all | solution.py:148
  385.1 11.8 %gather_fusion = bf16[1024,2048]{1,0:T(8,128)(2,1)} fusion(bf16[1152,2048]{1,0:T(8,128)(2,1)} %bitcast.21, s32[1024]{0:T(1024)S(1)} %broadcast_clamp_fusion), kind=kCustom, calls=%fused_computation | custom fusion | bytes 8392704 | tf_op jit(solution)/shard_map/gather | solution.py:149
  396.9 6.5 %fusion = f32[128,2048]{1,0:T(8,128)S(1)} fusion(bf16[1024,2048]{1,0:T(8,128)(2,1)} %gather_fusion, f32[128,8]{1,0:T(8,128)S(1)} %copy.64), kind=kLoop, calls=%fused_computation.3 | loop fusion | flops 6029312 | bytes 5246976 | tf_op jit(solution)/shard_map/reduce_sum | solution.py:150
  (111 shorter events, 44.4 us)
Async XLA Ops:
  6.5 273.0 %copy-start = (bf16[2048,16]{0,1:T(8,128)(2,1)S(1)}, bf16[2048,16]{0,1:T(8,128)(2,1)}, u32[]{:S(2)}) copy-start(bf16[2048,16]{0,1:T(8,128)(2,1)} %param.23) | copy-start | bytes 196612
  6.5 23.9 %copy-start.8 = (f32[128]{0:T(128)S(1)}, f32[128]{0:T(128)}, u32[]{:S(2)}) copy-start(f32[128]{0:T(128)} %param.18) | copy-start | bytes 1540
  6.5 64.2 %all-gather.5.cloned.1.call-start = ((), (), s32[]{:S(2)}) async-start(), calls=%async_computation.2 | async-start | bytes 6291456 | tf_op jit(solution)/shard_map/all_gather | solution.py:115
  7.3 115.5 %reduce-scatter.2.cloned.1.call-start = ((), (), s32[]{:S(2)}) async-start(), calls=%async_computation.3 | async-start | bytes 5242880 | tf_op jit(solution)/shard_map/reduce_scatter | solution.py:126
  77.2 47.2 %copy-start.5 = (f32[2048]{0:T(1024)S(1)}, f32[2048]{0:T(1024)}, u32[]{:S(2)}) copy-start(f32[2048]{0:T(1024)} %param.22) | copy-start | bytes 24580
  77.3 166.0 %all-gather.7.cloned.1.call-start = ((), (), s32[]{:S(2)}) async-start(), calls=%async_computation.4 | async-start | bytes 4718592 | tf_op jit(solution)/shard_map/all_gather | solution.py:119
  78.0 174.2 %all-gather.9.cloned.1.call-start = ((), (), s32[]{:S(2)}) async-start(), calls=%async_computation.5 | async-start | bytes 4718592 | tf_op jit(solution)/shard_map/all_gather | solution.py:120
  78.6 183.7 %all-gather.11.cloned.1.call-start = ((), (), s32[]{:S(2)}) async-start(), calls=%async_computation.6 | async-start | bytes 4718592 | tf_op jit(solution)/shard_map/all_gather | solution.py:121
  140.3 15.7 %collective-permute-start = (bf16[1,72,2048]{2,1,0:T(8,128)(2,1)}, bf16[1,72,2048]{2,1,0:T(8,128)(2,1)}, u32[]{:S(2)}, u32[]{:S(2)}) collective-permute-start(bf16[1,72,2048]{2,1,0:T(8,128)(2,1)} %get-tuple-element.23), channel_id=1, source_target_pairs={{0,1},{1,0},{2,3},{3,2},{4,5},{5,4},{6,7},{7,6},{8,9},{9,8},{10,11... | collective-permute-start | bytes 884744 | tf_op jit(solution)/shard_map/ppermute | solution.py:20
  141.8 23.8 %collective-permute-start.1 = (bf16[1,72,2048]{2,1,0:T(8,128)(2,1)}, bf16[1,72,2048]{2,1,0:T(8,128)(2,1)}, u32[]{:S(2)}, u32[]{:S(2)}) collective-permute-start(bf16[1,72,2048]{2,1,0:T(8,128)(2,1)} %get-tuple-element.22), channel_id=1, source_target_pairs={{0,2},{1,3},{2,0},{3,1},{4,6},{5,7},{6,4},{7,5},{8,10},{9,11},{10,... | collective-permute-start | bytes 884744 | tf_op jit(solution)/shard_map/ppermute | solution.py:20
  144.3 23.1 %collective-permute-start.2 = (bf16[1,72,2048]{2,1,0:T(8,128)(2,1)}, bf16[1,72,2048]{2,1,0:T(8,128)(2,1)S(1)}, u32[]{:S(2)}, u32[]{:S(2)}) collective-permute-start(bf16[1,72,2048]{2,1,0:T(8,128)(2,1)} %get-tuple-element.21), channel_id=1, source_target_pairs={{0,3},{1,2},{2,1},{3,0},{4,7},{5,6},{6,5},{7,4},{8,11},{9,10},{10,... | collective-permute-start | bytes 884744 | tf_op jit(solution)/shard_map/ppermute | solution.py:20
  144.8 24.0 %collective-permute-start.3 = (bf16[1,72,2048]{2,1,0:T(8,128)(2,1)}, bf16[1,72,2048]{2,1,0:T(8,128)(2,1)S(1)}, u32[]{:S(2)}, u32[]{:S(2)}) collective-permute-start(bf16[1,72,2048]{2,1,0:T(8,128)(2,1)} %get-tuple-element.20), channel_id=1, source_target_pairs={{0,4},{1,5},{2,6},{3,7},{4,0},{5,1},{6,2},{7,3},{8,12},{9,13},{10,... | collective-permute-start | bytes 884744 | tf_op jit(solution)/shard_map/ppermute | solution.py:20
  144.8 43.3 %collective-permute-start.4 = (bf16[1,72,2048]{2,1,0:T(8,128)(2,1)}, bf16[1,72,2048]{2,1,0:T(8,128)(2,1)S(1)}, u32[]{:S(2)}, u32[]{:S(2)}) collective-permute-start(bf16[1,72,2048]{2,1,0:T(8,128)(2,1)} %get-tuple-element.19), channel_id=1, source_target_pairs={{0,5},{1,4},{2,7},{3,6},{4,1},{5,0},{6,3},{7,2},{8,13},{9,12},{10,... | collective-permute-start | bytes 884744 | tf_op jit(solution)/shard_map/ppermute | solution.py:20
  156.0 35.3 %collective-permute-start.5 = (bf16[1,72,2048]{2,1,0:T(8,128)(2,1)}, bf16[1,72,2048]{2,1,0:T(8,128)(2,1)S(1)}, u32[]{:S(2)}, u32[]{:S(2)}) collective-permute-start(bf16[1,72,2048]{2,1,0:T(8,128)(2,1)} %get-tuple-element.18), channel_id=1, source_target_pairs={{0,6},{1,7},{2,4},{3,5},{4,2},{5,3},{6,0},{7,1},{8,14},{9,15},{10,... | collective-permute-start | bytes 884744 | tf_op jit(solution)/shard_map/ppermute | solution.py:20
  165.7 28.8 %collective-permute-start.6 = (bf16[1,72,2048]{2,1,0:T(8,128)(2,1)}, bf16[1,72,2048]{2,1,0:T(8,128)(2,1)S(1)}, u32[]{:S(2)}, u32[]{:S(2)}) collective-permute-start(bf16[1,72,2048]{2,1,0:T(8,128)(2,1)} %get-tuple-element.17), channel_id=1, source_target_pairs={{0,7},{1,6},{2,5},{3,4},{4,3},{5,2},{6,1},{7,0},{8,15},{9,14},{10,... | collective-permute-start | bytes 884744 | tf_op jit(solution)/shard_map/ppermute | solution.py:20
  167.4 37.8 %collective-permute-start.7 = (bf16[1,72,2048]{2,1,0:T(8,128)(2,1)}, bf16[1,72,2048]{2,1,0:T(8,128)(2,1)S(1)}, u32[]{:S(2)}, u32[]{:S(2)}) collective-permute-start(bf16[1,72,2048]{2,1,0:T(8,128)(2,1)} %get-tuple-element.16), channel_id=1, source_target_pairs={{0,8},{1,9},{2,10},{3,11},{4,12},{5,13},{6,14},{7,15},{8,0},{9,1},... | collective-permute-start | bytes 884744 | tf_op jit(solution)/shard_map/ppermute | solution.py:20
  168.7 43.5 %collective-permute-start.8 = (bf16[1,72,2048]{2,1,0:T(8,128)(2,1)}, bf16[1,72,2048]{2,1,0:T(8,128)(2,1)S(1)}, u32[]{:S(2)}, u32[]{:S(2)}) collective-permute-start(bf16[1,72,2048]{2,1,0:T(8,128)(2,1)} %get-tuple-element.15), channel_id=1, source_target_pairs={{0,9},{1,8},{2,11},{3,10},{4,13},{5,12},{6,15},{7,14},{8,1},{9,0},... | collective-permute-start | bytes 884744 | tf_op jit(solution)/shard_map/ppermute | solution.py:20
  188.1 28.2 %collective-permute-start.9 = (bf16[1,72,2048]{2,1,0:T(8,128)(2,1)S(1)}, bf16[1,72,2048]{2,1,0:T(8,128)(2,1)S(1)}, u32[]{:S(2)}, u32[]{:S(2)}) collective-permute-start(bf16[1,72,2048]{2,1,0:T(8,128)(2,1)S(1)} %get-tuple-element.14), channel_id=1, source_target_pairs={{0,10},{1,11},{2,8},{3,9},{4,14},{5,15},{6,12},{7,13},{8,2},{9,3},... | collective-permute-start | bytes 884744 | tf_op jit(solution)/shard_map/ppermute | solution.py:20
  191.3 25.8 %collective-permute-start.10 = (bf16[1,72,2048]{2,1,0:T(8,128)(2,1)S(1)}, bf16[1,72,2048]{2,1,0:T(8,128)(2,1)S(1)}, u32[]{:S(2)}, u32[]{:S(2)}) collective-permute-start(bf16[1,72,2048]{2,1,0:T(8,128)(2,1)S(1)} %get-tuple-element.13), channel_id=1, source_target_pairs={{0,11},{1,10},{2,9},{3,8},{4,15},{5,14},{6,13},{7,12},{8,3},{9,2},... | collective-permute-start | bytes 884744 | tf_op jit(solution)/shard_map/ppermute | solution.py:20
  194.5 29.2 %collective-permute-start.11 = (bf16[1,72,2048]{2,1,0:T(8,128)(2,1)S(1)}, bf16[1,72,2048]{2,1,0:T(8,128)(2,1)S(1)}, u32[]{:S(2)}, u32[]{:S(2)}) collective-permute-start(bf16[1,72,2048]{2,1,0:T(8,128)(2,1)S(1)} %get-tuple-element.12), channel_id=1, source_target_pairs={{0,12},{1,13},{2,14},{3,15},{4,8},{5,9},{6,10},{7,11},{8,4},{9,5},... | collective-permute-start | bytes 884744 | tf_op jit(solution)/shard_map/ppermute | solution.py:20
  205.2 19.2 %collective-permute-start.12 = (bf16[1,72,2048]{2,1,0:T(8,128)(2,1)S(1)}, bf16[1,72,2048]{2,1,0:T(8,128)(2,1)S(1)}, u32[]{:S(2)}, u32[]{:S(2)}) collective-permute-start(bf16[1,72,2048]{2,1,0:T(8,128)(2,1)S(1)} %get-tuple-element.11), channel_id=1, source_target_pairs={{0,13},{1,12},{2,15},{3,14},{4,9},{5,8},{6,11},{7,10},{8,5},{9,4},... | collective-permute-start | bytes 884744 | tf_op jit(solution)/shard_map/ppermute | solution.py:20
  212.3 29.6 %collective-permute-start.13 = (bf16[1,72,2048]{2,1,0:T(8,128)(2,1)S(1)}, bf16[1,72,2048]{2,1,0:T(8,128)(2,1)S(1)}, u32[]{:S(2)}, u32[]{:S(2)}) collective-permute-start(bf16[1,72,2048]{2,1,0:T(8,128)(2,1)S(1)} %get-tuple-element.10), channel_id=1, source_target_pairs={{0,14},{1,15},{2,12},{3,13},{4,10},{5,11},{6,8},{7,9},{8,6},{9,7},... | collective-permute-start | bytes 884744 | tf_op jit(solution)/shard_map/ppermute | solution.py:20
  216.3 26.2 %collective-permute-start.14 = (bf16[1,72,2048]{2,1,0:T(8,128)(2,1)S(1)}, bf16[1,72,2048]{2,1,0:T(8,128)(2,1)S(1)}, u32[]{:S(2)}, u32[]{:S(2)}) collective-permute-start(bf16[1,72,2048]{2,1,0:T(8,128)(2,1)S(1)} %get-tuple-element.9), channel_id=1, source_target_pairs={{0,15},{1,14},{2,13},{3,12},{4,11},{5,10},{6,9},{7,8},{8,7},{9,6},... | collective-permute-start | bytes 884744 | tf_op jit(solution)/shard_map/ppermute | solution.py:20
  269.7 115.5 %all-to-all-start = ((bf16[16,72,2048]{2,1,0:T(8,128)(2,1)}), bf16[16,72,2048]{2,1,0:T(8,128)(2,1)}, u32[]{:S(2)}, u32[]{:S(2)}) async-start(bf16[16,72,2048]{2,1,0:T(8,128)(2,1)} %bitcast.104), calls=%async_computation.1 | async-start | bytes 9437184 | tf_op jit(solution)/shard_map/all_to_all | solution.py:148
  (6 other events, 28.5 us)
Sparse Core Ops, SparseCore 0:
  8.9 61.7 all-gather.4
  77.4 45.3 reduce-scatter.1
  124.4 44.9 all-gather.6
  170.8 44.9 all-gather.8
  217.3 44.9 all-gather.10
